TPU v7x, 32 devices: a whole 2x2x4 slice. The times are simulated.
32 devices in a mesh: grp: 8 (over y, x, core), rep: 4 (over z).
Axes of the slice: x: 2, y: 2, z: 4, core: 2. Of those that a mesh axis runs over, the one named last changes fastest.
Arguments:
- features: bfloat16 [4096, 256], P(('grp', 'rep')), may hold values from -0.0625 to 0.0625
- weight: bfloat16 [256, 256], replicated, may hold values from -0.375 to 0.375
- preact: bfloat16 [4096, 256], P(('grp', 'rep')), may hold values from -6 to 6
- grad_out: bfloat16 [4096, 256], P(('grp', 'rep')), may hold values from -1.5 to 1.5
- degree: int32 [4096], P(('grp', 'rep')), may hold values from 1 to 64
- tile_values: bfloat16 [256, 4, 128, 128], P(('grp', 'rep')), may hold values from 0 to 1
- tile_rows: int32 [256, 4], P(('grp', 'rep')), may hold values from -1 to 3, as said below
Outputs:
- input_grad: float32 [4096, 256], P(('grp', 'rep'))
- weight_grad: float32 [256, 256], replicated
Inputs may be any that keep to these rules, and one draw needn't show every extreme that they name: `tile_rows`: each of the 8 rows of one device (aligned blocks) has up to 4 live slots; in every such block some row has all 4 slots live.
All inputs are finite; a program needn't handle non-finite values.
Results may differ from a plain program's by a relative error of at most 0.013.
Values may be sent and summed in bfloat16 or wider, within the bound.
No kernel may reach another device: no remote copies, remote signals or barrier semaphores. Data moves between devices by JAX's collectives and lax.ppermute only.
A program may use at most 128 MiB of HBM per device.

v0:
```python
import jax
import jax.numpy as jnp
from jax import lax
from jax.sharding import PartitionSpec as P


def tile_masks(tile_rows):
    tile_live = tile_rows >= 0
    clipped = jnp.where(tile_live, tile_rows, 0)
    return (tile_live, clipped)


def per_device(features, weight, preact, grad_out, degree, tile_values, tile_rows):
    rows_here = features.shape[0]
    feature_width = features.shape[1]
    tile_edge = tile_values.shape[2]
    slot_count = tile_values.shape[1]
    row_tiles = lax.axis_size("rep") * rows_here // tile_edge
    inverse = lax.rsqrt(degree.astype(jnp.float32))[:, None]
    grad_pre = jnp.where(preact > 0, grad_out, jnp.zeros_like(grad_out))
    tile_live, clipped = tile_masks(tile_rows)
    scaled = (features.astype(jnp.float32) * inverse).astype(jnp.bfloat16)
    gathered = lax.all_gather(scaled, "grp", axis=0, tiled=True)
    columns = gathered.reshape(-1, tile_edge, feature_width)
    target = jnp.where(tile_live, tile_rows, row_tiles)
    partial_value = jnp.zeros((row_tiles + 1, tile_edge, feature_width), jnp.float32)
    for slot in range(slot_count):
        product = jnp.einsum(
            "cij,cjf->cif", tile_values[:, slot], columns, preferred_element_type=jnp.float32
        )
        partial_value = partial_value.at[target[:, slot]].add(product)
    partial_value = partial_value[:row_tiles]
    summed = lax.psum_scatter(
        partial_value.reshape(row_tiles * tile_edge, feature_width).astype(jnp.bfloat16),
        "rep",
        scatter_dimension=0,
        tiled=True,
    ).astype(jnp.float32)
    aggregated = (summed * inverse).astype(jnp.bfloat16)
    weight_local = lax.dot_general(
        aggregated, grad_pre, (((0,), (0,)), ((), ())), preferred_element_type=jnp.float32
    )
    projected = (
        lax.dot_general(
            grad_pre, weight, (((1,), (1,)), ((), ())), preferred_element_type=jnp.float32
        )
        * inverse
    ).astype(jnp.bfloat16)
    block_rows = lax.all_gather(projected, "rep", axis=0, tiled=True)
    blocks = block_rows.reshape(row_tiles, tile_edge, feature_width)
    picked = jnp.take(blocks, clipped, axis=0)
    picked = jnp.where(tile_live[:, :, None, None], picked, jnp.zeros_like(picked))
    result = jnp.einsum("csij,csif->cjf", tile_values, picked, preferred_element_type=jnp.float32)
    input_grad = (
        lax.psum_scatter(
            result.reshape(rows_here * lax.axis_size("grp"), feature_width),
            "grp",
            scatter_dimension=0,
            tiled=True,
        )
        * inverse
    )
    weight_grad = lax.psum(weight_local, ("grp", "rep"))
    return (input_grad, weight_grad)


def solution(mesh):
    return jax.shard_map(
        per_device,
        mesh=mesh,
        in_specs=(
            P(("grp", "rep"), None),
            P(),
            P(("grp", "rep"), None),
            P(("grp", "rep"), None),
            P(("grp", "rep")),
            P(("grp", "rep"), None, None, None),
            P(("grp", "rep"), None),
        ),
        out_specs=(P(("grp", "rep"), None), P()),
        check_vma=False,
    )
```

profile of v0, /device:TPU:0, one launch (start us, length us, event | category | flops | bytes accessed | tf_op | source)
XLA Modules:
  0.0 254.5 jit_solution(7141739193772190387)
XLA Ops:
  7.2 0.0 copy-start
  7.2 0.0 reduce-scatter.3.cloned.1.call-start
  7.2 0.7 broadcast_select_fusion
  7.9 0.7 broadcast_compare_fusion
  8.6 0.7 convert_rsqrt_fusion
  9.3 0.0 copy-done
  9.3 1.1 fusion.5
  10.4 15.6 %all_gather.6 = bf16[512,256]{1,0:T(8,128)(2,1)S(1)} all-gather(bf16[128,256]{1,0:T(8,128)(2,1)S(1)} %fusion.5), channel_id=1, replica_groups=mesh['grp'=8,'rep'=4] {'rep'}, dimensions={0}, use_global_device_ids=true | all-gather | bytes 327680 | tf_op jit(solution)/shard_map/all_gather | solution.py:49
  26.0 0.1 copy.27
  26.1 0.1 reshape.27
  26.2 0.1 copy.25
  26.3 0.7 copy.26
  26.9 0.7 gather_fusion
  27.6 0.5 copy-done.1
  28.1 2.4 fusion
  30.5 0.0 reduce-scatter.3.cloned.1.call-update
  30.5 0.0 reduce-scatter.5.cloned.1.call-start
  30.6 0.5 fusion.21
  31.1 37.1 %reduce-scatter.3.cloned.1.call-done = f32[128,256]{1,0:T(8,128)} async-done(((f32[1024,256]{1,0:T(8,128)}), f32[128,256]{1,0:T(8,128)}) %reduce-scatter.3.cloned.1.call-update) | async-done | bytes 131088 | tf_op jit(solution)/shard_map/reduce_scatter | solution.py:55
  68.2 0.0 copy-done.4
  68.3 1.6 multiply_convert_fusion.1
  69.9 9.8 %all_gather.7 = bf16[1024,256]{1,0:T(8,128)(2,1)S(1)} all-gather(bf16[128,256]{1,0:T(8,128)(2,1)S(1)} %get-tuple-element.10), channel_id=1, replica_groups=mesh['grp'=8,'rep'=4] {'grp'}, dimensions={0}, use_global_device_ids=true | all-gather | bytes 589824 | tf_op jit(solution)/shard_map/all_gather | solution.py:23
  79.7 1.4 convolution_bitcast_fusion.3
  81.1 0.3 convolution_bitcast_fusion.2
  81.4 0.3 convolution_bitcast_fusion.1
  81.8 1.3 convolution_bitcast_fusion
  83.1 2.6 %copy.31 = f32[8,128,256]{2,1,0:T(8,128)} copy(f32[8,128,256]{1,2,0:T(8,128)} %convolution_bitcast_fusion.3) | data formatting | bytes 2097152 | tf_op jit(solution)/shard_map/cij,cjf->cif/dot_general | solution.py:28
  85.6 1.4 copy.34
  87.0 0.3 copy.37
  87.3 0.3 copy.40
  87.7 0.0 copy-start.5
  87.7 0.0 copy-done.6
  87.7 2.5 scatter_fusion
  90.2 0.0 copy-done.5
  90.2 2.5 scatter_fusion.1
  92.7 1.3 scatter_fusion.2
  94.0 0.0 copy-start.2
  94.0 0.0 copy-start.3
  94.0 1.3 scatter_fusion.3
  95.4 0.7 slice.61
  96.1 0.0 reduce-scatter.5.cloned.1.call-update
  96.1 0.0 all-reduce.2.cloned.1.call-start
  96.2 19.8 %reduce-scatter.5.cloned.1.call-done = bf16[128,256]{1,0:T(8,128)(2,1)} async-done(((bf16[512,256]{1,0:T(8,128)(2,1)}), bf16[128,256]{1,0:T(8,128)(2,1)}) %reduce-scatter.5.cloned.1.call-update) | async-done | bytes 65552 | tf_op jit(solution)/shard_map/reduce_scatter | solution.py:33
  115.9 0.0 copy-done.3
  115.9 1.8 fusion.16
  117.8 0.0 all-reduce.2.cloned.1.call-update
  117.8 128.5 %all-reduce.2.cloned.1.call-done = f32[256,256]{1,0:T(8,128)} async-done(((f32[256,256]{1,0:T(8,128)}), f32[256,256]{1,0:T(8,128)}) %all-reduce.2.cloned.1.call-update) | async-done | bytes 262160 | tf_op jit(solution)/shard_map/psum | solution.py:63
  246.3 1.7 copy.56
  (6 shorter events, 0.1 us)
Async XLA Ops:
  7.2 2.1 copy-start
  7.2 61.1 %reduce-scatter.3.cloned.1.call-start = ((), (), s32[]{:S(2)}) async-start(), calls=%async_computation.2 | async-start | bytes 1179648 | tf_op jit(solution)/shard_map/reduce_scatter | solution.py:55
  26.9 1.2 copy-start.1
  28.1 40.1 %copy-start.4 = (bf16[128,256]{1,0:T(8,128)(2,1)S(1)}, bf16[128,256]{1,0:T(8,128)(2,1)}, u32[]{:S(2)}) copy-start(bf16[128,256]{1,0:T(8,128)(2,1)} %param.7) | copy-start | bytes 196612
  30.5 85.4 %reduce-scatter.5.cloned.1.call-start = ((), (), s32[]{:S(2)}) async-start(), calls=%async_computation.3 | async-start | bytes 327680 | tf_op jit(solution)/shard_map/reduce_scatter | solution.py:33
  87.0 0.8 copy-start.6
  87.7 2.5 %copy-start.5 = (s32[8]{0:T(128)S(1)}, s32[8]{0:T(128)}, u32[]{:S(2)}) copy-start(s32[8]{0:T(128)} %get-tuple-element.4) | copy-start | bytes 100
  94.0 21.9 %copy-start.2 = (bf16[128,256]{1,0:T(8,128)(2,1)S(1)}, bf16[128,256]{1,0:T(8,128)(2,1)}, u32[]{:S(2)}) copy-start(bf16[128,256]{1,0:T(8,128)(2,1)} %param.10) | copy-start | bytes 196612
  94.0 21.9 %copy-start.3 = (bf16[128,256]{1,0:T(8,128)(2,1)S(1)}, bf16[128,256]{1,0:T(8,128)(2,1)}, u32[]{:S(2)}) copy-start(bf16[128,256]{1,0:T(8,128)(2,1)} %param.9) | copy-start | bytes 196612
  96.1 150.1 %all-reduce.2.cloned.1.call-start = ((), (), s32[]{:S(2)}) async-start(), calls=%async_computation.4 | async-start | bytes 524288 | tf_op jit(solution)/shard_map/psum | solution.py:63
Sparse Core Ops, SparseCore 0:
  30.7 37.5 reduce-scatter.2
  96.3 19.6 reduce-scatter.4
  122.9 123.2 all-reduce.1
where the time goes:
time: 255 us; the launch traced here: 254 us
  waiting for transfers between devices  185 us (73%)
  blocking collectives  25.4 us (10%)
  between operations  13.9 us (5%)
  other arithmetic  11.8 us (5%)
  local copies, waits for them, and re-layouts  9.19 us (4%)
  matrix products  8.64 us (3%)
    psum x1, waiting for transfers between devices, per_device(): weight_grad = lax.psum(weight_local, ('grp', 'rep'))  128 us
    reduce_scatter x1, waiting for transfers between devices, per_device(): lax.psum_scatter(result.reshape(rows_here * lax.axis_size('grp'), feature...  37.1 us
    reduce_scatter x1, waiting for transfers between devices, per_device(): lax.psum_scatter(partial_value.reshape(row_tiles * tile_edge, feature_wid...  19.8 us
    all_gather x1, blocking collectives, per_device(): block_rows = lax.all_gather(projected, 'rep', axis=0, tiled=True)  15.6 us
    all_gather x1, blocking collectives, per_device(): gathered = lax.all_gather(scaled, 'grp', axis=0, tiled=True)  9.77 us
    scatter-add x4, other arithmetic, per_device(): partial_value = partial_value.at[target[:, slot]].add(product)  7.56 us
  transfers between devices with their start and end apart: 3, of which 3 were waited for; matrix products, arithmetic and copies ran while one was open for 0% of the time, Pallas kernels for 0%

commit v1 on v0

--- a/solution.py
+++ b/solution.py
@@ -2,6 +2,19 @@
 import jax.numpy as jnp
 from jax import lax
 from jax.sharding import PartitionSpec as P
+
+
+def gather_around(x, axis, dim):
+    ways = lax.axis_size(axis)
+    up = [(d, (d + 1) % ways) for d in range(ways)]
+    down = [(d, (d - 1) % ways) for d in range(ways)]
+    earlier, later = ([x], [x])
+    for _ in range(ways // 2):
+        earlier.append(lax.ppermute(earlier[-1], axis, up))
+    for _ in range((ways - 1) // 2):
+        later.append(lax.ppermute(later[-1], axis, down))
+    line = jnp.concatenate([*earlier[::-1], *later[1:]], axis=dim)
+    return jnp.roll(line, (lax.axis_index(axis) - ways // 2) * x.shape[dim], axis=dim)
 
 
 def tile_masks(tile_rows):
@@ -20,7 +33,7 @@
     grad_pre = jnp.where(preact > 0, grad_out, jnp.zeros_like(grad_out))
     tile_live, clipped = tile_masks(tile_rows)
     scaled = (features.astype(jnp.float32) * inverse).astype(jnp.bfloat16)
-    gathered = lax.all_gather(scaled, "grp", axis=0, tiled=True)
+    gathered = gather_around(scaled, "grp", 0)
     columns = gathered.reshape(-1, tile_edge, feature_width)
     target = jnp.where(tile_live, tile_rows, row_tiles)
     partial_value = jnp.zeros((row_tiles + 1, tile_edge, feature_width), jnp.float32)

time: 255 us -> 266 us (1.043)
  waiting for transfers between devices: 185 us -> 198 us
  blocking collectives: 25.4 us -> 15.6 us
  starting transfers between devices: 0.12 us -> 8.06 us
    ppermute x0 -> x7, waiting for transfers between devices: none -> 11 us  [the longest x4 10.5 us: gather_around(): earlier.append(lax.ppermute(earlier[-1], axis, up))]
    all_gather x1 -> x0, blocking collectives: 9.77 us -> none  [per_device(): gathered = lax.all_gather(scaled, 'grp', axis=0, tiled=True)]
    ppermute x0 -> x7, starting transfers between devices: none -> 7.94 us  [the longest x3 7.93 us: gather_around(): later.append(lax.ppermute(later[-1], axis, down))]
  transfers between devices with their start and end apart: 3 -> 10, of which waited for: 3 -> 8; matrix products, arithmetic and copies ran while one was open for 0% -> 0% of each run, Pallas kernels for 0% -> 0%
where the time goes in v1:
time: 266 us
  waiting for transfers between devices  198 us (74%)
  blocking collectives  15.6 us (6%)
  between operations  14 us (5%)
  other arithmetic  11.9 us (4%)
  local copies, waits for them, and re-layouts  9.33 us (4%)
  matrix products  8.61 us (3%)
  starting transfers between devices  8.06 us (3%)
    psum x1, waiting for transfers between devices, per_device(): weight_grad = lax.psum(weight_local, ('grp', 'rep'))  128 us
    reduce_scatter x1, waiting for transfers between devices, per_device(): lax.psum_scatter(result.reshape(rows_here * lax.axis_size('grp'), feature...  37.7 us
    reduce_scatter x1, waiting for transfers between devices, per_device(): lax.psum_scatter(partial_value.reshape(row_tiles * tile_edge, feature_wid...  21 us
    all_gather x1, blocking collectives, per_device(): block_rows = lax.all_gather(projected, 'rep', axis=0, tiled=True)  15.6 us
    ppermute x4, waiting for transfers between devices, gather_around(): earlier.append(lax.ppermute(earlier[-1], axis, up))  10.5 us
    ppermute x3, starting transfers between devices, gather_around(): later.append(lax.ppermute(later[-1], axis, down))  7.93 us
    scatter-add x4, other arithmetic, per_device(): partial_value = partial_value.at[target[:, slot]].add(product)  7.56 us
  transfers between devices with their start and end apart: 10, of which 8 were waited for; matrix products, arithmetic and copies ran while one was open for 0% of the time, Pallas kernels for 0%

profile of v1, /device:TPU:0, one launch (start us, length us, event | category | flops | bytes accessed | tf_op | source)
XLA Modules:
  0.0 265.6 jit_solution(17707081738039124069)
XLA Ops:
  7.2 0.0 copy-start
  7.2 0.0 reduce-scatter.3.cloned.1.call-start
  7.2 0.7 broadcast_select_fusion
  7.9 0.7 broadcast_compare_fusion
  8.6 0.7 convert_rsqrt_fusion
  9.3 1.1 fusion.5
  10.4 15.6 %all_gather.3 = bf16[512,256]{1,0:T(8,128)(2,1)S(1)} all-gather(bf16[128,256]{1,0:T(8,128)(2,1)S(1)} %fusion.5), channel_id=1, replica_groups=mesh['grp'=8,'rep'=4] {'rep'}, dimensions={0}, use_global_device_ids=true | all-gather | bytes 327680 | tf_op jit(solution)/shard_map/all_gather | solution.py:62
  26.0 0.1 copy.23
  26.1 0.1 reshape.27
  26.2 0.1 copy.21
  26.3 0.7 copy.22
  26.9 0.7 gather_fusion
  27.6 0.5 copy-done.1
  28.1 2.3 fusion
  30.5 0.0 reduce-scatter.3.cloned.1.call-update
  30.5 0.0 reduce-scatter.5.cloned.1.call-start
  30.6 37.7 %reduce-scatter.3.cloned.1.call-done = f32[128,256]{1,0:T(8,128)} async-done(((f32[1024,256]{1,0:T(8,128)}), f32[128,256]{1,0:T(8,128)}) %reduce-scatter.3.cloned.1.call-update) | async-done | bytes 131088 | tf_op jit(solution)/shard_map/reduce_scatter | solution.py:68
  68.2 1.6 multiply_convert_fusion.1
  69.9 4.6 %collective-permute-done = bf16[128,256]{1,0:T(8,128)(2,1)S(1)} collective-permute-done((bf16[128,256]{1,0:T(8,128)(2,1)S(1)}, bf16[128,256]{1,0:T(8,128)(2,1)S(1)}, u32[]{:S(2)}, u32[]{:S(2)}) %collective-permute-start) | collective-permute-done | bytes 65568 | tf_op jit(solution)/shard_map/ppermute | solution.py:13
  74.5 2.6 collective-permute-start.4
  77.1 2.6 collective-permute-done.1
  79.7 2.6 collective-permute-start.5
  82.4 2.0 collective-permute-done.2
  84.3 0.6 fusion.21
  84.9 2.6 collective-permute-start.6
  87.6 1.4 collective-permute-done.3
  89.0 0.5 collective-permute-done.6
  89.6 1.4 convolution_bitcast_fusion.3
  91.0 0.3 convolution_bitcast_fusion.2
  91.4 0.3 convolution_bitcast_fusion.1
  91.7 1.3 convolution_bitcast_fusion
  93.0 2.5 copy.27
  95.6 1.4 copy.30
  96.9 0.3 copy.33
  97.3 0.3 copy.36
  97.6 0.0 copy-start.5
  97.7 2.5 scatter_fusion
  100.2 2.5 scatter_fusion.1
  102.6 1.3 scatter_fusion.2
  104.0 1.3 scatter_fusion.3
  105.3 0.7 slice.61
  106.1 0.0 reduce-scatter.5.cloned.1.call-update
  106.1 0.0 all-reduce.2.cloned.1.call-start
  106.1 21.0 %reduce-scatter.5.cloned.1.call-done = bf16[128,256]{1,0:T(8,128)(2,1)} async-done(((bf16[512,256]{1,0:T(8,128)(2,1)}), bf16[128,256]{1,0:T(8,128)(2,1)}) %reduce-scatter.5.cloned.1.call-update) | async-done | bytes 65552 | tf_op jit(solution)/shard_map/reduce_scatter | solution.py:46
  127.1 1.8 fusion.16
  129.0 0.0 all-reduce.2.cloned.1.call-update
  129.0 128.4 %all-reduce.2.cloned.1.call-done = f32[256,256]{1,0:T(8,128)} async-done(((f32[256,256]{1,0:T(8,128)}), f32[256,256]{1,0:T(8,128)}) %all-reduce.2.cloned.1.call-update) | async-done | bytes 262160 | tf_op jit(solution)/shard_map/psum | solution.py:76
  257.4 1.7 copy.67
  (36 shorter events, 0.2 us)
Async XLA Ops:
  7.2 2.1 copy-start
  7.2 61.1 %reduce-scatter.3.cloned.1.call-start = ((), (), s32[]{:S(2)}) async-start(), calls=%async_computation.2 | async-start | bytes 1179648 | tf_op jit(solution)/shard_map/reduce_scatter | solution.py:68
  26.9 1.2 copy-start.1
  28.1 40.1 %copy-start.4 = (bf16[128,256]{1,0:T(8,128)(2,1)S(1)}, bf16[128,256]{1,0:T(8,128)(2,1)}, u32[]{:S(2)}) copy-start(bf16[128,256]{1,0:T(8,128)(2,1)} %param.7) | copy-start | bytes 196612
  30.5 96.6 %reduce-scatter.5.cloned.1.call-start = ((), (), s32[]{:S(2)}) async-start(), calls=%async_computation.3 | async-start | bytes 327680 | tf_op jit(solution)/shard_map/reduce_scatter | solution.py:46
  69.9 4.6 %collective-permute-start = (bf16[128,256]{1,0:T(8,128)(2,1)S(1)}, bf16[128,256]{1,0:T(8,128)(2,1)S(1)}, u32[]{:S(2)}, u32[]{:S(2)}) collective-permute-start(bf16[128,256]{1,0:T(8,128)(2,1)S(1)} %get-tuple-element.10), channel_id=1, source_target_pairs={{0,4},{4,8},{8,12},{12,16},{16,20},{20,24},{24,28},{28,0},{1,5},{5... | collective-permute-start | bytes 196616 | tf_op jit(solution)/shard_map/ppermute | solution.py:13
  74.5 5.2 %collective-permute-start.1 = (bf16[128,256]{1,0:T(8,128)(2,1)S(1)}, bf16[128,256]{1,0:T(8,128)(2,1)S(1)}, u32[]{:S(2)}, u32[]{:S(2)}) collective-permute-start(bf16[128,256]{1,0:T(8,128)(2,1)S(1)} %collective-permute-done), channel_id=1, source_target_pairs={{0,4},{4,8},{8,12},{12,16},{16,20},{20,24},{24,28},{28,0},{1,5},{5... | collective-permute-start | bytes 196616 | tf_op jit(solution)/shard_map/ppermute | solution.py:13
  74.5 5.2 %collective-permute-start.4 = (bf16[128,256]{1,0:T(8,128)(2,1)S(1)}, bf16[128,256]{1,0:T(8,128)(2,1)S(1)}, u32[]{:S(2)}, u32[]{:S(2)}) collective-permute-start(bf16[128,256]{1,0:T(8,128)(2,1)S(1)} %get-tuple-element.10), channel_id=1, source_target_pairs={{0,28},{4,0},{8,4},{12,8},{16,12},{20,16},{24,20},{28,24},{1,29},{... | collective-permute-start | bytes 196616 | tf_op jit(solution)/shard_map/ppermute | solution.py:15
  79.7 4.6 %collective-permute-start.2 = (bf16[128,256]{1,0:T(8,128)(2,1)S(1)}, bf16[128,256]{1,0:T(8,128)(2,1)S(1)}, u32[]{:S(2)}, u32[]{:S(2)}) collective-permute-start(bf16[128,256]{1,0:T(8,128)(2,1)S(1)} %collective-permute-done.1), channel_id=1, source_target_pairs={{0,4},{4,8},{8,12},{12,16},{16,20},{20,24},{24,28},{28,0},{1,5},{5... | collective-permute-start | bytes 196616 | tf_op jit(solution)/shard_map/ppermute | solution.py:13
  79.7 5.2 %collective-permute-start.5 = (bf16[128,256]{1,0:T(8,128)(2,1)S(1)}, bf16[128,256]{1,0:T(8,128)(2,1)S(1)}, u32[]{:S(2)}, u32[]{:S(2)}) collective-permute-start(bf16[128,256]{1,0:T(8,128)(2,1)S(1)} %collective-permute-done.4), channel_id=1, source_target_pairs={{0,28},{4,0},{8,4},{12,8},{16,12},{20,16},{24,20},{28,24},{1,29},{... | collective-permute-start | bytes 196616 | tf_op jit(solution)/shard_map/ppermute | solution.py:15
  84.3 4.6 %collective-permute-start.3 = (bf16[128,256]{1,0:T(8,128)(2,1)S(1)}, bf16[128,256]{1,0:T(8,128)(2,1)S(1)}, u32[]{:S(2)}, u32[]{:S(2)}) collective-permute-start(bf16[128,256]{1,0:T(8,128)(2,1)S(1)} %collective-permute-done.2), channel_id=1, source_target_pairs={{0,4},{4,8},{8,12},{12,16},{16,20},{20,24},{24,28},{28,0},{1,5},{5... | collective-permute-start | bytes 196616 | tf_op jit(solution)/shard_map/ppermute | solution.py:13
  84.9 4.5 %collective-permute-start.6 = (bf16[128,256]{1,0:T(8,128)(2,1)S(1)}, bf16[128,256]{1,0:T(8,128)(2,1)S(1)}, u32[]{:S(2)}, u32[]{:S(2)}) collective-permute-start(bf16[128,256]{1,0:T(8,128)(2,1)S(1)} %collective-permute-done.5), channel_id=1, source_target_pairs={{0,28},{4,0},{8,4},{12,8},{16,12},{20,16},{24,20},{28,24},{1,29},{... | collective-permute-start | bytes 196616 | tf_op jit(solution)/shard_map/ppermute | solution.py:15
  96.9 0.8 copy-start.6
  97.6 2.5 copy-start.5
  104.0 23.2 %copy-start.2 = (bf16[128,256]{1,0:T(8,128)(2,1)S(1)}, bf16[128,256]{1,0:T(8,128)(2,1)}, u32[]{:S(2)}) copy-start(bf16[128,256]{1,0:T(8,128)(2,1)} %param.10) | copy-start | bytes 196612
  104.0 23.2 %copy-start.3 = (bf16[128,256]{1,0:T(8,128)(2,1)S(1)}, bf16[128,256]{1,0:T(8,128)(2,1)}, u32[]{:S(2)}) copy-start(bf16[128,256]{1,0:T(8,128)(2,1)} %param.9) | copy-start | bytes 196612
  106.1 151.3 %all-reduce.2.cloned.1.call-start = ((), (), s32[]{:S(2)}) async-start(), calls=%async_computation.4 | async-start | bytes 524288 | tf_op jit(solution)/shard_map/psum | solution.py:76
Sparse Core Ops, SparseCore 0:
  30.6 37.5 reduce-scatter.2
  106.2 20.8 reduce-scatter.4
  134.1 123.2 all-reduce.1
